TPU v7x, 128 devices: a whole 4x4x4 slice. The times are simulated.
128 devices in a mesh: aux: 4 (over x), row: 32 (over z, y, core).
Axes of the slice: x: 4, y: 4, z: 4, core: 2. Of those that a mesh axis runs over, the one named last changes fastest.
Arguments:
- b_tiles: bfloat16 [4, 32768, 2048], P('aux', 'row'), may hold values from -0.125 to 0.125
- occ_coeff: bfloat16 [32768, 256], P('row'), may hold values from -3 to 3
- tile_blocks: int32 [256, 16], P('row'), may hold values from 0 to 255, as said below
- screen_mask: int32 [256, 16], P('row'), may hold values from 0 to 1, as said below
Outputs:
- exchange: bfloat16 [32768, 32, 4, 256], P('row', None, 'aux')
Inputs may be any that keep to these rules, and one draw needn't show every extreme that they name: `tile_blocks`: each entry names a basis block at most 8 blocks away from its own row's block; the first slot of every block names the block itself. `screen_mask`: in every basis block the kept slots come first; some block keeps all 16.
All inputs are finite; a program needn't handle non-finite values.
Results may differ from a plain program's by a relative error of at most 0.0057.
Values may be sent and summed in bfloat16 or wider, within the bound.
No kernel may reach another device: no remote copies, remote signals or barrier semaphores. Data moves between devices by JAX's collectives and lax.ppermute only.
A program may use at most 128 MiB of HBM per device.

v0:
```python
import jax
import jax.numpy as jnp
from jax import lax
from jax.sharding import PartitionSpec as P


def with_halo(block, sides, width):
    for axis, dim in sides:
        count = lax.axis_size(axis)
        forward = [(i, i + 1) for i in range(count - 1)]
        backward = [(target, source) for source, target in forward]
        low = lax.ppermute(
            lax.slice_in_dim(block, block.shape[dim] - width, None, axis=dim), axis, forward
        )
        high = lax.ppermute(lax.slice_in_dim(block, 0, width, axis=dim), axis, backward)
        block = jnp.concatenate([low, block, high], axis=dim)
    return block


def per_device(b_tiles, occ_coeff, tile_blocks, screen_mask):
    p_local, rows_local, stored = b_tiles.shape
    blocks_local, slot_count = tile_blocks.shape
    block_size = rows_local // blocks_local
    orbitals = occ_coeff.shape[1]
    row_count = lax.axis_size("row")
    aux_count = lax.axis_size("aux")
    extended = with_halo(occ_coeff, (("row", 0),), rows_local)
    coeff_blocks = extended.reshape(3 * blocks_local, block_size, orbitals)
    local_index = tile_blocks - (lax.axis_index("row") - 1) * blocks_local
    picked = jnp.take(coeff_blocks, local_index, axis=0)
    keep_mask = screen_mask.astype(jnp.bfloat16)
    tiles_five = b_tiles.reshape(p_local, blocks_local, block_size, slot_count, block_size)
    masked = picked * keep_mask[:, :, None, None]
    half_sum = jnp.einsum(
        "pbmsn,bsni->pbmi", tiles_five, masked, preferred_element_type=jnp.float32
    )
    half_local = half_sum.astype(jnp.bfloat16).reshape(p_local, rows_local, orbitals)
    slab_rows = lax.all_gather(half_local, "aux", axis=0, tiled=True)
    share = rows_local // aux_count
    all_rows = lax.all_gather(half_local, "row", axis=1, tiled=True)
    split_rows = all_rows.reshape(p_local, row_count, aux_count, share, orbitals)
    regrouped = lax.all_to_all(split_rows, "aux", split_axis=2, concat_axis=0, tiled=True)
    partner = regrouped.reshape(p_local * aux_count, row_count * share, orbitals)
    result = jnp.einsum("pmi,pli->ml", slab_rows, partner, preferred_element_type=jnp.float32)
    return result.astype(jnp.bfloat16).reshape(rows_local, row_count, 1, share)


def solution(mesh):
    in_specs = (P("aux", "row", None), P("row", None), P("row", None), P("row", None))
    out_specs = P("row", None, "aux", None)
    return jax.shard_map(
        per_device, mesh=mesh, in_specs=in_specs, out_specs=out_specs, check_vma=False
    )
```

profile of v0, /device:TPU:1, one launch (start us, length us, event | category | flops | bytes accessed | tf_op | source)
XLA Modules:
  0.0 382.9 jit_solution(15495398956538830125)
XLA Ops:
  7.4 0.0 copy-start
  7.4 0.0 copy-start.1
  7.4 0.0 all-gather.5.cloned.1.call-start
  7.4 4.7 %collective-permute-start = (bf16[1024,256]{1,0:T(8,128)(2,1)}, bf16[1024,256]{1,0:T(8,128)(2,1)S(1)}, u32[]{:S(2)}, u32[]{:S(2)}) collective-permute-start(bf16[1024,256]{1,0:T(8,128)(2,1)} %param.5), channel_id=1, source_target_pairs={{0,1},{1,2},{2,3},{3,4},{4,5},{5,6},{6,7},{7,8},{8,9},{9,10},{10,1... | collective-permute-start | bytes 1572872 | tf_op jit(solution)/shard_map/ppermute | solution.py:12
  12.1 1.9 collective-permute-start.1
  14.0 0.7 compare_and_fusion
  14.7 0.1 reshape.37
  14.8 5.6 %copy.12 = bf16[128,8,16,128]{3,2,1,0:T(8,128)(2,1)} copy(bf16[128,8,16,128]{3,1,2,0:T(8,128)(2,1)} %bitcast.36) | data formatting | bytes 8388608
  20.4 0.0 copy-done.1
  20.4 0.0 collective-permute-done
  20.4 2.4 collective-permute-done.1
  22.8 0.0 copy-done
  22.8 0.1 pad_maximum_fusion
  22.9 6.7 %gather_fusion = bf16[128,128,256]{2,1,0:T(8,128)(2,1)} fusion(bf16[24,128,256]{2,1,0:T(8,128)(2,1)S(1)} %bitcast.32, s32[1024]{0:T(1024)S(1)} %pad_clamp_fusion), kind=kCustom, calls=%fused_computation | custom fusion | bytes 16777728 | tf_op jit(solution)/shard_map/jit(_take)/gather | solution.py:30
  29.7 8.2 %fusion.12 = bf16[8,256,128]{1,2,0:T(8,128)(2,1)} fusion(bf16[8,16,128,256]{3,2,1,0:T(8,128)(2,1)} %bitcast.35, pred[8,16]{1,0:T(8,128)(4,1)S(1)} %get-tuple-element.5, bf16[8,16]{1,0:T(8,128)(2,1)S(1)} %convert_element_type.15, bf16[8,128,16,128]{3,2,1,0:T(8,128)(2,1)} %bitcast.37), kind=kOutput, calls=%fused_computation.11 | convolution fusion | flops 1094975488 | bytes 13107584 | tf_op jit(solution)/shard_map/pbmsn,bsni->pbmi/dot_general | solution.py:34
  37.8 0.0 all-gather.5.cloned.1.call-update
  37.9 76.5 %all-gather.5.cloned.1.call-done = bf16[1,32768,256]{2,1,0:T(8,128)(2,1)} async-done(((bf16[1,1024,256]{2,1,0:T(8,128)(2,1)}), bf16[1,32768,256]{2,1,0:T(8,128)(2,1)}) %all-gather.5.cloned.1.call-update) | async-done | bytes 16777232 | tf_op jit(solution)/shard_map/all_gather | solution.py:40
  114.4 14.0 %copy.9 = bf16[1,32,4,256,256]{4,3,1,0,2:T(8,128)(2,1)} copy(bf16[1,32,4,256,256]{4,3,2,1,0:T(8,128)(2,1)} %bitcast.33) | data formatting | bytes 33554432 | tf_op jit(solution)/shard_map/reshape | solution.py:41
  128.3 7.0 %all-to-all-start = ((bf16[1,32,4,256,256]{4,3,1,0,2:T(8,128)(2,1)}), bf16[1,32,4,256,256]{4,3,1,0,2:T(8,128)(2,1)}, u32[]{:S(2)}, u32[]{:S(2)}) async-start(bf16[1,32,4,256,256]{4,3,1,0,2:T(8,128)(2,1)} %copy.9), calls=%async_computation | async-start | bytes 33554432 | tf_op jit(solution)/shard_map/all_to_all | solution.py:42
  135.3 0.0 all-gather.3.cloned.1.call-start
  135.4 0.5 all-gather.3.cloned.1.call-update
  135.9 48.8 %all-gather.3.cloned.1.call-done = bf16[4,1024,256]{2,1,0:T(8,128)(2,1)} async-done(((bf16[1,1024,256]{2,1,0:T(8,128)(2,1)}), bf16[4,1024,256]{2,1,0:T(8,128)(2,1)}) %all-gather.3.cloned.1.call-update) | async-done | bytes 2097168 | tf_op jit(solution)/shard_map/all_gather | solution.py:38
  184.8 151.0 %all-to-all-done = bf16[1,32,4,256,256]{4,3,1,0,2:T(8,128)(2,1)} async-done(((bf16[1,32,4,256,256]{4,3,1,0,2:T(8,128)(2,1)}), bf16[1,32,4,256,256]{4,3,1,0,2:T(8,128)(2,1)}, u32[]{:S(2)}, u32[]{:S(2)}) %all-to-all-start) | async-done | bytes 16777248 | tf_op jit(solution)/shard_map/all_to_all | solution.py:42
  335.8 24.1 %bitcast_convert_fusion = bf16[1024,8192]{1,0:T(8,128)(2,1)} fusion(bf16[4,1024,256]{2,1,0:T(8,128)(2,1)} %all-gather.3.cloned.1.call-done, bf16[4,8192,256]{2,1,0:T(8,128)(2,1)} %bitcast.12), kind=kOutput, calls=%fused_computation.1 | convolution fusion | flops 17188257792 | bytes 35651584 | tf_op jit(solution)/shard_map/pmi,pli->ml/dot_general | solution.py:44
  359.8 15.6 %copy.13 = bf16[128,8,32,256]{3,2,1,0:T(8,128)(2,1)} copy(bf16[128,8,32,256]{3,1,2,0:T(8,128)(2,1)} %bitcast.34) | data formatting | bytes 33554432
  (2 shorter events, 0.0 us)
Async XLA Ops:
  7.4 15.4 %copy-start = (bf16[1024,256]{1,0:T(8,128)(2,1)S(1)}, bf16[1024,256]{1,0:T(8,128)(2,1)}, u32[]{:S(2)}) copy-start(bf16[1024,256]{1,0:T(8,128)(2,1)} %param.5) | copy-start | bytes 1572868
  7.4 13.0 %copy-start.1 = (s32[8,16]{1,0:T(8,128)S(1)}, s32[8,16]{1,0:T(8,128)}, u32[]{:S(2)}) copy-start(s32[8,16]{1,0:T(8,128)} %param.7) | copy-start | bytes 1540
  7.4 107.0 %all-gather.5.cloned.1.call-start = ((), (), s32[]{:S(2)}) async-start(), calls=%async_computation.2 | async-start | bytes 17301504 | tf_op jit(solution)/shard_map/all_gather | solution.py:40
  7.4 13.0 %collective-permute-start = (bf16[1024,256]{1,0:T(8,128)(2,1)}, bf16[1024,256]{1,0:T(8,128)(2,1)S(1)}, u32[]{:S(2)}, u32[]{:S(2)}) collective-permute-start(bf16[1024,256]{1,0:T(8,128)(2,1)} %param.5), channel_id=1, source_target_pairs={{0,1},{1,2},{2,3},{3,4},{4,5},{5,6},{6,7},{7,8},{8,9},{9,10},{10,1... | collective-permute-start | bytes 1572872 | tf_op jit(solution)/shard_map/ppermute | solution.py:12
  12.1 10.7 %collective-permute-start.1 = (bf16[1024,256]{1,0:T(8,128)(2,1)}, bf16[1024,256]{1,0:T(8,128)(2,1)S(1)}, u32[]{:S(2)}, u32[]{:S(2)}) collective-permute-start(bf16[1024,256]{1,0:T(8,128)(2,1)} %param.5), channel_id=1, source_target_pairs={{1,0},{2,1},{3,2},{4,3},{5,4},{6,5},{7,6},{8,7},{9,8},{10,9},{11,1... | collective-permute-start | bytes 1572872 | tf_op jit(solution)/shard_map/ppermute | solution.py:15
  128.3 207.4 %all-to-all-start = ((bf16[1,32,4,256,256]{4,3,1,0,2:T(8,128)(2,1)}), bf16[1,32,4,256,256]{4,3,1,0,2:T(8,128)(2,1)}, u32[]{:S(2)}, u32[]{:S(2)}) async-start(bf16[1,32,4,256,256]{4,3,1,0,2:T(8,128)(2,1)} %copy.9), calls=%async_computation | async-start | bytes 33554432 | tf_op jit(solution)/shard_map/all_to_all | solution.py:42
  135.3 49.4 %all-gather.3.cloned.1.call-start = ((), (), s32[]{:S(2)}) async-start(), calls=%async_computation.1 | async-start | bytes 2621440 | tf_op jit(solution)/shard_map/all_gather | solution.py:38
Sparse Core Ops, SparseCore 0:
  38.0 76.3 all-gather.4
Sparse Core Ops, SparseCore 1:
  137.5 47.2 all-gather.2
where the time goes:
time: 383 us
  waiting for transfers between devices  279 us (73%)
  local copies, waits for them, and re-layouts  42 us (11%)
  matrix products  32.2 us (8%)
  between operations  14.9 us (4%)
  starting transfers between devices  13.7 us (4%)
    all_to_all x1, waiting for transfers between devices, per_device(): lax.all_to_all(split_rows, 'aux', split_axis=2, concat_axis=0, tiled=True)  151 us
    all_gather x1, waiting for transfers between devices, per_device(): all_rows = lax.all_gather(half_local, 'row', axis=1, tiled=True)  76.5 us
    all_gather x1, waiting for transfers between devices, per_device(): slab_rows = lax.all_gather(half_local, 'aux', axis=0, tiled=True)  48.8 us
    dot_general x1, matrix products, per_device(): jnp.einsum('pmi,pli->ml', slab_rows, partner, preferred_element_type=jnp....  24.1 us
    unnamed x6, local copies, waits for them, and re-layouts  21.2 us
    reshape x1, local copies, waits for them, and re-layouts, per_device(): all_rows.reshape(p_local, row_count, aux_count, share, orbitals)  14 us
    dot_general x1, matrix products, per_device(): jnp.einsum('pbmsn,bsni->pbmi', tiles_five, masked, preferred_element_type...  8.17 us
  transfers between devices with their start and end apart: 5, of which 4 were waited for; matrix products, arithmetic and copies ran while one was open for 2% of the time, Pallas kernels for 0%

commit v1 on v0

--- a/solution.py
+++ b/solution.py
@@ -37,7 +37,13 @@
     half_local = half_sum.astype(jnp.bfloat16).reshape(p_local, rows_local, orbitals)
     slab_rows = lax.all_gather(half_local, "aux", axis=0, tiled=True)
     share = rows_local // aux_count
-    all_rows = lax.all_gather(half_local, "row", axis=1, tiled=True)
+
+    def launch_block_up(xs, device_axis, dimension_no):
+        fresh = jnp.stack([xs for _ in range(lax.axis_size(device_axis))], 0)
+        y1 = lax.all_to_all(fresh, device_axis, 0, 0)
+        return jnp.concatenate(y1, dimension_no)
+
+    all_rows = launch_block_up(half_local, "row", 1)
     split_rows = all_rows.reshape(p_local, row_count, aux_count, share, orbitals)
     regrouped = lax.all_to_all(split_rows, "aux", split_axis=2, concat_axis=0, tiled=True)
     partner = regrouped.reshape(p_local * aux_count, row_count * share, orbitals)

time: 383 us -> 494 us (1.29)
  blocking collectives: 0 us -> 195 us
  waiting for transfers between devices: 279 us -> 203 us
  local copies, waits for them, and re-layouts: 42 us -> 36.5 us
    all_to_all x0 -> x1, blocking collectives: none -> 195 us  [launch_block_up(): y1 = lax.all_to_all(fresh, device_axis, 0, 0)]
    all_gather x1 -> x0, waiting for transfers between devices: 76.5 us -> none  [per_device(): all_rows = lax.all_gather(half_local, 'row', axis=1, tiled=True)]
    reshape x1 -> x0, local copies, waits for them, and re-layouts: 14 us -> none  [per_device(): all_rows.reshape(p_local, row_count, aux_count, share, orbitals)]
    another operation x0 -> x2, local copies, waits for them, and re-layouts: none -> 8.5 us  [the longest x1 6.53 us: per_device(): all_rows.reshape(p_local, row_count, aux_count, share, orbitals)]
    unnamed x6 -> x8, local copies, waits for them, and re-layouts: 21.2 us -> 21.2 us
  transfers between devices with their start and end apart: 5 -> 4, of which waited for: 4 -> 3; matrix products, arithmetic and copies ran while one was open for 2% -> 1% of each run, Pallas kernels for 0% -> 0%
where the time goes in v1:
time: 494 us
  waiting for transfers between devices  203 us (41%)
  blocking collectives  195 us (39%)
  local copies, waits for them, and re-layouts  36.5 us (7%)
  matrix products  31.4 us (6%)
  starting transfers between devices  13.7 us (3%)
  between operations  13.5 us (3%)
    all_to_all x1, blocking collectives, launch_block_up(): y1 = lax.all_to_all(fresh, device_axis, 0, 0)  195 us
    all_to_all x1, waiting for transfers between devices, per_device(): lax.all_to_all(split_rows, 'aux', split_axis=2, concat_axis=0, tiled=True)  149 us
    all_gather x1, waiting for transfers between devices, per_device(): slab_rows = lax.all_gather(half_local, 'aux', axis=0, tiled=True)  50.8 us
    dot_general x1, matrix products, per_device(): jnp.einsum('pmi,pli->ml', slab_rows, partner, preferred_element_type=jnp....  24.1 us
    unnamed x8, local copies, waits for them, and re-layouts  21.2 us
  transfers between devices with their start and end apart: 4, of which 3 were waited for; matrix products, arithmetic and copies ran while one was open for 1% of the time, Pallas kernels for 0%

profile of v1, /device:TPU:1, one launch (start us, length us, event | category | flops | bytes accessed | tf_op | source)
XLA Modules:
  0.0 493.7 jit_solution(1522438948736765495)
XLA Ops:
  6.5 0.0 copy-start.1
  6.5 0.0 copy-start.2
  6.5 4.7 collective-permute-start
  11.3 1.9 collective-permute-start.1
  13.2 0.7 compare_and_fusion
  13.9 0.1 reshape.37
  14.0 5.6 %copy.14 = bf16[128,8,16,128]{3,2,1,0:T(8,128)(2,1)} copy(bf16[128,8,16,128]{3,1,2,0:T(8,128)(2,1)} %bitcast.38) | data formatting | bytes 8388608
  19.5 0.0 copy-done.2
  19.5 0.0 collective-permute-done
  19.6 2.4 collective-permute-done.1
  22.0 0.0 copy-done.1
  22.0 0.1 pad_maximum_fusion
  22.1 6.7 %gather_fusion = bf16[128,128,256]{2,1,0:T(8,128)(2,1)} fusion(bf16[24,128,256]{2,1,0:T(8,128)(2,1)S(1)} %bitcast.35, s32[1024]{0:T(1024)S(1)} %pad_clamp_fusion), kind=kCustom, calls=%fused_computation | custom fusion | bytes 16777728 | tf_op jit(solution)/shard_map/jit(_take)/gather | solution.py:30
  28.8 7.3 %fusion.12 = bf16[8,256,128]{1,2,0:T(8,128)(2,1)S(1)} fusion(bf16[8,16,128,256]{3,2,1,0:T(8,128)(2,1)} %bitcast.37, pred[8,16]{1,0:T(8,128)(4,1)S(1)} %get-tuple-element.5, bf16[8,16]{1,0:T(8,128)(2,1)S(1)} %convert_element_type.15, bf16[8,128,16,128]{3,2,1,0:T(8,128)(2,1)} %bitcast.39), kind=kOutput, calls=%fused_computation.11 | convolution fusion | flops 1094975488 | bytes 13107584 | tf_op jit(solution)/shard_map/pbmsn,bsni->pbmi/dot_general | solution.py:34
  36.2 0.0 copy-start
  36.2 2.0 stack.3
  38.2 0.0 copy-done
  38.2 195.2 %all_to_all.20 = bf16[32,1,1024,256]{3,2,1,0:T(8,128)(2,1)S(1)} all-to-all(bf16[32,1,1024,256]{3,2,1,0:T(8,128)(2,1)S(1)} %stack.3), channel_id=1, replica_groups=mesh['aux'=4,'row'=32] {'row'}, dimensions={0} | all-to-all | bytes 33554432 | tf_op jit(solution)/shard_map/all_to_all | solution.py:43
  233.4 6.5 %copy.11 = bf16[1,32,4,256,256]{4,3,1,0,2:T(8,128)(2,1)} copy(bf16[1,32,4,256,256]{4,3,2,1,0:T(8,128)(2,1)S(1)} %bitcast.34) | data formatting | bytes 33554432 | tf_op jit(solution)/shard_map/reshape;reshape | solution.py:47
  239.9 7.0 %all-to-all-start.1 = ((bf16[1,32,4,256,256]{4,3,1,0,2:T(8,128)(2,1)}), bf16[1,32,4,256,256]{4,3,1,0,2:T(8,128)(2,1)}, u32[]{:S(2)}, u32[]{:S(2)}) async-start(bf16[1,32,4,256,256]{4,3,1,0,2:T(8,128)(2,1)} %copy.11), calls=%async_computation.1 | async-start | bytes 33554432 | tf_op jit(solution)/shard_map/all_to_all | solution.py:48
  246.9 0.0 all-gather.2.cloned.1.call-start
  246.9 0.7 all-gather.2.cloned.1.call-update
  247.6 50.8 %all-gather.2.cloned.1.call-done = bf16[4,1024,256]{2,1,0:T(8,128)(2,1)} async-done(((bf16[1,1024,256]{2,1,0:T(8,128)(2,1)}), bf16[4,1024,256]{2,1,0:T(8,128)(2,1)}) %all-gather.2.cloned.1.call-update) | async-done | bytes 2097168 | tf_op jit(solution)/shard_map/all_gather | solution.py:38
  298.4 148.8 %all-to-all-done.1 = bf16[1,32,4,256,256]{4,3,1,0,2:T(8,128)(2,1)} async-done(((bf16[1,32,4,256,256]{4,3,1,0,2:T(8,128)(2,1)}), bf16[1,32,4,256,256]{4,3,1,0,2:T(8,128)(2,1)}, u32[]{:S(2)}, u32[]{:S(2)}) %all-to-all-start.1) | async-done | bytes 16777248 | tf_op jit(solution)/shard_map/all_to_all | solution.py:48
  447.1 24.1 %bitcast_convert_fusion = bf16[1024,8192]{1,0:T(8,128)(2,1)} fusion(bf16[4,1024,256]{2,1,0:T(8,128)(2,1)} %all-gather.2.cloned.1.call-done, bf16[4,8192,256]{2,1,0:T(8,128)(2,1)} %bitcast.12), kind=kOutput, calls=%fused_computation.1 | convolution fusion | flops 17188257792 | bytes 35651584 | tf_op jit(solution)/shard_map/pmi,pli->ml/dot_general | solution.py:50
  471.2 15.6 %copy.15 = bf16[128,8,32,256]{3,2,1,0:T(8,128)(2,1)} copy(bf16[128,8,32,256]{3,1,2,0:T(8,128)(2,1)} %bitcast.36) | data formatting | bytes 33554432
  (2 shorter events, 0.0 us)
Async XLA Ops:
  6.5 15.4 %copy-start.1 = (bf16[1024,256]{1,0:T(8,128)(2,1)S(1)}, bf16[1024,256]{1,0:T(8,128)(2,1)}, u32[]{:S(2)}) copy-start(bf16[1024,256]{1,0:T(8,128)(2,1)} %param.5) | copy-start | bytes 1572868
  6.5 13.0 %copy-start.2 = (s32[8,16]{1,0:T(8,128)S(1)}, s32[8,16]{1,0:T(8,128)}, u32[]{:S(2)}) copy-start(s32[8,16]{1,0:T(8,128)} %param.7) | copy-start | bytes 1540
  6.5 13.0 %collective-permute-start = (bf16[1024,256]{1,0:T(8,128)(2,1)}, bf16[1024,256]{1,0:T(8,128)(2,1)S(1)}, u32[]{:S(2)}, u32[]{:S(2)}) collective-permute-start(bf16[1024,256]{1,0:T(8,128)(2,1)} %param.5), channel_id=1, source_target_pairs={{0,1},{1,2},{2,3},{3,4},{4,5},{5,6},{6,7},{7,8},{8,9},{9,10},{10,1... | collective-permute-start | bytes 1572872 | tf_op jit(solution)/shard_map/ppermute | solution.py:12
  11.3 10.7 %collective-permute-start.1 = (bf16[1024,256]{1,0:T(8,128)(2,1)}, bf16[1024,256]{1,0:T(8,128)(2,1)S(1)}, u32[]{:S(2)}, u32[]{:S(2)}) collective-permute-start(bf16[1024,256]{1,0:T(8,128)(2,1)} %param.5), channel_id=1, source_target_pairs={{1,0},{2,1},{3,2},{4,3},{5,4},{6,5},{7,6},{8,7},{9,8},{10,9},{11,1... | collective-permute-start | bytes 1572872 | tf_op jit(solution)/shard_map/ppermute | solution.py:15
  36.2 2.0 copy-start
  239.9 207.3 %all-to-all-start.1 = ((bf16[1,32,4,256,256]{4,3,1,0,2:T(8,128)(2,1)}), bf16[1,32,4,256,256]{4,3,1,0,2:T(8,128)(2,1)}, u32[]{:S(2)}, u32[]{:S(2)}) async-start(bf16[1,32,4,256,256]{4,3,1,0,2:T(8,128)(2,1)} %copy.11), calls=%async_computation.1 | async-start | bytes 33554432 | tf_op jit(solution)/shard_map/all_to_all | solution.py:48
  246.9 51.5 %all-gather.2.cloned.1.call-start = ((), (), s32[]{:S(2)}) async-start(), calls=%async_computation.2 | async-start | bytes 2621440 | tf_op jit(solution)/shard_map/all_gather | solution.py:38
Sparse Core Ops, SparseCore 0:
  249.4 48.9 all-gather.1
